TPU v7x, 32 devices: a whole 2x2x4 slice. The times are simulated.
32 devices in a mesh: req: 8 (over z, x), kv: 4 (over y, core).
Axes of the slice: x: 2, y: 2, z: 4, core: 2. Of those that a mesh axis runs over, the one named last changes fastest.
Arguments:
- activations: bfloat16 [4992, 2048], P('req', 'kv'), may hold values from -6 to 6
- span_length: int32 [104], P('req'), may hold values from 1 to 48, as said below
- offsets: int32 [104], P('req'), may hold values from 64 to 8191
- decode_slot: int32 [104], P('req'), may hold values from 0 to 103, as said below
- attention_gain: float32 [2048], replicated, may hold values from 0.1 to 1.9
- query_weight: bfloat16 [2048, 2048], P(None, 'kv'), may hold values from -0.125 to 0.125
- key_projection_matrix: bfloat16 [2048, 1024], P(None, 'kv'), may hold values from -0.125 to 0.125
- value_projection_matrix: bfloat16 [2048, 1024], P(None, 'kv'), may hold values from -0.125 to 0.125
- output_weight: bfloat16 [2048, 2048], P('kv'), may hold values from -0.125 to 0.125
- feedforward_gain: float32 [2048], replicated, may hold values from 0.1 to 1.9
- gate_weight: bfloat16 [2048, 4096], P(None, 'kv'), may hold values from -0.125 to 0.125
- up_weight: bfloat16 [2048, 4096], P(None, 'kv'), may hold values from -0.125 to 0.125
- down_weight: bfloat16 [4096, 2048], P('kv'), may hold values from -0.09375 to 0.09375
- earlier_rotated_keys: bfloat16 [104, 64, 1024], P('req', 'kv'), may hold values from -300 to 300
- earlier_values: bfloat16 [104, 64, 1024], P('req', 'kv'), may hold values from -6 to 6
Outputs:
- layer_out: bfloat16 [4992, 2048], P('req', 'kv')
- decode_keys: bfloat16 [104, 64, 1024], P('req', None, 'kv')
- decode_values: bfloat16 [104, 64, 1024], P('req', None, 'kv')
Inputs may be any that keep to these rules, and one draw needn't show every extreme that they name: `span_length`: on some prefill device every request fills all 48 positions. `decode_slot`: each slot appears once; decode device d owns slots d * 13 to (d + 1) * 13 - 1; at most 2 requests of one prefill device go to one decode device; every prefill device p sends exactly 2 requests to decode device p + 1 (counted round); the differences of decode device minus prefill device, modulo the number of devices of req, form the same multiset on every prefill device.
All inputs are finite; a program needn't handle non-finite values.
Results may differ from a plain program's by a relative error of at most 0.012.
Values may be sent and summed in bfloat16 or wider, within the bound.
No kernel may reach another device: no remote copies, remote signals or barrier semaphores. Data moves between devices by JAX's collectives and lax.ppermute only.
A program may use at most 128 MiB of HBM per device.

v0:
```python
import math
import jax
import jax.numpy as jnp
from jax import lax
from jax.sharding import Mesh
from jax.sharding import PartitionSpec as P

HEAD_WIDTH = 256
CORES = 2
rope_base = 1000042.0
epsilon = 1e-05


def rotate_pairs(tensor, position):
    half_size = tensor.shape[-1] // 2
    steps_float = jnp.arange(half_size, dtype=jnp.float32)
    inverse = jnp.exp(steps_float * (-2.0 * math.log(rope_base) / tensor.shape[-1]))
    angles = position[:, :, None] * inverse[None, None, :]
    cosine = jnp.cos(angles)[:, :, None, :]
    sine_part = jnp.sin(angles)[:, :, None, :]
    first_half = tensor[..., :half_size]
    second = tensor[..., half_size:]
    return jnp.concatenate(
        [first_half * cosine - second * sine_part, second * cosine + first_half * sine_part],
        axis=-1,
    )


def allowed_keys(span_length, span_size, past_size):
    key_pos = jnp.arange(past_size + span_size, dtype=jnp.int32) - past_size
    query_pos = jnp.arange(span_size, dtype=jnp.int32)
    causal = key_pos[None, :] <= query_pos[:, None]
    live_keys = key_pos[None, None, :] < span_length[:, None, None]
    return (key_pos[None, None, :] < 0) | causal[None, :, :] & live_keys


def gather_features(share):
    chips = lax.axis_size("kvy")
    rows, width = share.shape
    pair = lax.all_gather(share, "kvy", axis=1, tiled=True)
    whole = lax.all_gather(pair, "core", axis=1, tiled=True)
    whole = whole.reshape(rows, CORES, chips, width).transpose(0, 2, 1, 3)
    return whole.reshape(rows, CORES * chips * width)


def swap_blocks(matrix):
    chips = lax.axis_size("kvy")
    rows, cols = matrix.shape
    width = cols // (CORES * chips)
    return matrix.reshape(rows, chips, CORES, width).transpose(0, 2, 1, 3).reshape(rows, cols)


def scatter_features(partial):
    on_chip = lax.psum_scatter(partial, "core", scatter_dimension=1, tiled=True)
    return lax.psum_scatter(on_chip, "kvy", scatter_dimension=1, tiled=True)


def row_scale(values, gain_share):
    square_sum = lax.psum(jnp.sum(values * values, axis=-1, keepdims=True), ("kvy", "core"))
    width = values.shape[-1] * lax.axis_size("kvy") * CORES
    return values * lax.rsqrt(square_sum / width + epsilon) * gain_share


def local(
    activations,
    span_length,
    offsets,
    decode_slot,
    attention_gain,
    query_weight,
    key_projection_matrix,
    value_projection_matrix,
    output_weight,
    feedforward_gain,
    gate_weight,
    up_weight,
    down_weight,
    earlier_rotated_keys,
    earlier_values,
):
    req_count = lax.axis_size("req")
    chips = lax.axis_size("kvy")
    kv_count = chips * CORES
    kv_index = lax.axis_index("kvy") * CORES + lax.axis_index("core")
    req_index = lax.axis_index("req")
    request_list = span_length.shape[0]
    total_rows, width_share = activations.shape
    span_size = total_rows // request_list
    local_kv = key_projection_matrix.shape[1] // HEAD_WIDTH
    local_q = query_weight.shape[1] // HEAD_WIDTH
    query_groups = local_q // local_kv
    past_share = earlier_rotated_keys.shape[1]
    stacked = jnp.stack([earlier_rotated_keys, earlier_values])
    stacked = stacked.reshape(2, request_list, past_share, kv_count, local_kv * HEAD_WIDTH)
    stacked = stacked.transpose(0, 3, 1, 2, 4)
    arrived = lax.all_to_all(stacked, ("kvy", "core"), split_axis=1, concat_axis=1, tiled=True)
    head_kv = arrived.transpose(0, 2, 1, 3, 4).reshape(
        2, request_list, kv_count * past_share, local_kv * HEAD_WIDTH
    )
    past_size = head_kv.shape[2]
    capacity = max(2, (request_list + req_count - 1) // req_count)
    order_ids = jnp.arange(request_list, dtype=jnp.int32)
    earlier = order_ids[None, :] < order_ids[:, None]
    own_dest = decode_slot // request_list
    same_dest = own_dest[:, None] == own_dest[None, :]
    own_rank = jnp.sum((same_dest & earlier).astype(jnp.int32), axis=1)
    buffer_place = own_dest * capacity + own_rank
    buffer_ids = jnp.arange(req_count * capacity, dtype=jnp.int32)
    matches = buffer_place[None, :] == buffer_ids[:, None]
    picked = jnp.sum(jnp.where(matches, order_ids[None, :], 0), axis=1)
    filled = jnp.any(matches, axis=1)
    packed = jnp.take(head_kv, picked, axis=1)
    packed = jnp.where(filled[None, :, None, None], packed, jnp.zeros((), packed.dtype))
    packed = packed.reshape((2, req_count, capacity) + packed.shape[2:])
    packed_slots = jnp.where(filled, jnp.take(decode_slot, picked), -1).reshape(req_count, capacity)
    landed = lax.all_to_all(packed, "req", split_axis=1, concat_axis=1, tiled=True)
    landed_slots = lax.all_to_all(packed_slots, "req", split_axis=0, concat_axis=0, tiled=True)
    wanted = req_index * request_list + order_ids
    slot_hits = landed_slots.reshape(1, -1) == wanted[:, None]
    entry_ids = jnp.arange(req_count * capacity, dtype=jnp.int32)
    slot_position = jnp.sum(jnp.where(slot_hits, entry_ids[None, :], 0), axis=1)
    landed = landed.reshape((2, req_count * capacity) + landed.shape[3:])
    decode_kv = jnp.take(landed, slot_position, axis=1)
    x_whole = gather_features(activations)
    x_float = x_whole.astype(jnp.float32)
    square_sum = jnp.sum(x_float * x_float, axis=-1, keepdims=True)
    normalized_input = (
        x_float * lax.rsqrt(square_sum / x_float.shape[-1] + epsilon) * attention_gain
    ).astype(jnp.bfloat16)
    position = (
        offsets[:, None].astype(jnp.float32) + jnp.arange(span_size, dtype=jnp.float32)[None, :]
    )
    query_rows = jnp.dot(
        normalized_input, query_weight, preferred_element_type=jnp.float32
    ).reshape(request_list, span_size, local_q, HEAD_WIDTH)
    query_rows = rotate_pairs(query_rows, position).astype(jnp.bfloat16)
    fresh_keys = jnp.dot(
        normalized_input, key_projection_matrix, preferred_element_type=jnp.float32
    ).reshape(request_list, span_size, local_kv, HEAD_WIDTH)
    fresh_keys = rotate_pairs(fresh_keys, position).astype(jnp.bfloat16)
    fresh_values = (
        jnp.dot(normalized_input, value_projection_matrix, preferred_element_type=jnp.float32)
        .astype(jnp.bfloat16)
        .reshape(request_list, span_size, local_kv, HEAD_WIDTH)
    )
    combined_keys = jnp.concatenate(
        [head_kv[0].reshape(request_list, past_size, local_kv, HEAD_WIDTH), fresh_keys], axis=1
    )
    combined_values = jnp.concatenate(
        [head_kv[1].reshape(request_list, past_size, local_kv, HEAD_WIDTH), fresh_values], axis=1
    )
    grouped_queries = query_rows.reshape(
        request_list, span_size, local_kv, query_groups, HEAD_WIDTH
    )
    scores = jnp.einsum(
        "rckgd,rskd->rkgcs", grouped_queries, combined_keys, preferred_element_type=jnp.float32
    ) / math.sqrt(HEAD_WIDTH)
    allowed = allowed_keys(span_length, span_size, past_size)[:, None, None, :, :]
    scores = jnp.where(allowed, scores, -jnp.inf)
    weights = jax.nn.softmax(scores, axis=-1).astype(jnp.bfloat16)
    mixed_heads = jnp.einsum(
        "rkgcs,rskd->rckgd", weights, combined_values, preferred_element_type=jnp.float32
    )
    mixed_heads = mixed_heads.astype(jnp.bfloat16).reshape(total_rows, local_q * HEAD_WIDTH)
    head_part = jnp.dot(mixed_heads, swap_blocks(output_weight), preferred_element_type=jnp.float32)
    head_share = scatter_features(head_part)
    residual_share = activations.astype(jnp.float32) + head_share
    gain_share = lax.dynamic_slice_in_dim(feedforward_gain, kv_index * width_share, width_share)
    normed_share = row_scale(residual_share, gain_share).astype(jnp.bfloat16)
    normed_two = gather_features(normed_share)
    gate_proj = jnp.dot(normed_two, gate_weight, preferred_element_type=jnp.float32)
    upward = jnp.dot(normed_two, up_weight, preferred_element_type=jnp.float32)
    hidden = (jax.nn.silu(gate_proj) * upward).astype(jnp.bfloat16)
    mlp_share = scatter_features(
        jnp.dot(hidden, swap_blocks(down_weight), preferred_element_type=jnp.float32)
    )
    live_rows = (jnp.arange(span_size, dtype=jnp.int32)[None, :] < span_length[:, None]).reshape(
        total_rows
    )
    layer_out = jnp.where(live_rows[:, None], residual_share + mlp_share, 0.0).astype(jnp.bfloat16)
    return (layer_out, decode_kv[0], decode_kv[1])


def solution(mesh):
    req_size, kv_size = mesh.devices.shape
    split_mesh = Mesh(
        mesh.devices.reshape(req_size, kv_size // CORES, CORES), ("req", "kvy", "core")
    )
    kv = ("kvy", "core")
    return jax.shard_map(
        local,
        mesh=split_mesh,
        in_specs=(
            P("req", kv),
            P("req"),
            P("req"),
            P("req"),
            P(),
            P(None, kv),
            P(None, kv),
            P(None, kv),
            P(kv, None),
            P(),
            P(None, kv),
            P(None, kv),
            P(kv, None),
            P("req", kv, None),
            P("req", kv, None),
        ),
        out_specs=(P("req", kv), P("req", None, kv), P("req", None, kv)),
        check_vma=False,
    )
```

profile of v0, /device:TPU:0, one launch (start us, length us, event | category | flops | bytes accessed | tf_op | source)
XLA Modules:
  0.0 338.3 jit_solution(16456305696777216266)
XLA Ops:
  8.0 28.2 %all-gather.5.cloned.1.call-done = bf16[624,1024]{1,0:T(8,128)(2,1)} async-done(((bf16[624,512]{1,0:T(8,128)(2,1)}), bf16[624,1024]{1,0:T(8,128)(2,1)}) %all-gather.5.cloned.1.call-update) | async-done | bytes 1277968 | tf_op jit(solution)/shard_map/all_gather | solution.py:40
  36.2 2.1 stack.10
  39.4 1.9 maximum_bitcast_fusion
  41.3 1.1 copy.111
  42.3 4.4 %all-to-all-start = ((bf16[2,4,13,16,256]{4,3,2,0,1:T(8,128)(2,1)}), bf16[2,4,13,16,256]{4,3,2,0,1:T(8,128)(2,1)}, u32[]{:S(2)}, u32[]{:S(2)}) async-start(bf16[2,4,13,16,256]{4,3,2,0,1:T(8,128)(2,1)} %copy.111), calls=%async_computation | async-start | bytes 1703936 | tf_op jit(solution)/shard_map/all_to_all | solution.py:96
  46.8 2.5 copy.132
  49.3 2.9 copy.120
  52.2 1.5 copy.121
  53.9 1.2 multiply_cosine_fusion
  55.1 4.0 %all-to-all-done = bf16[2,4,13,16,256]{4,3,2,0,1:T(8,128)(2,1)} async-done(((bf16[2,4,13,16,256]{4,3,2,0,1:T(8,128)(2,1)}), bf16[2,4,13,16,256]{4,3,2,0,1:T(8,128)(2,1)}, u32[]{:S(2)}, u32[]{:S(2)}) %all-to-all-start) | async-done | bytes 852000 | tf_op jit(solution)/shard_map/all_to_all | solution.py:96
  59.2 1.3 copy.136
  61.5 4.8 %copy.113 = f32[624,2048]{0,1:T(8,128)} copy(bf16[624,2048]{1,0:T(8,128)(2,1)} %all-gather.7.cloned.1.call-done) | data formatting | bytes 7667712 | tf_op jit(solution)/shard_map/convert_element_type | solution.py:125
  66.3 3.0 multiply_reduce_fusion
  69.3 8.9 %copy.115 = f32[624,2,2,512]{3,2,1,0:T(2,128)} copy(f32[624,2,2,512]{0,3,1,2:T(8,128)} %bitcast.105) | data formatting | bytes 10223616 | tf_op jit(solution)/shard_map/convert_element_type | solution.py:125
  78.2 5.1 %copy.114 = f32[624,2,2,512]{0,3,2,1:T(8,128)} copy(f32[624,2,2,512]{0,3,1,2:T(8,128)} %bitcast.106) | data formatting | bytes 10223616 | tf_op jit(solution)/shard_map/convert_element_type | solution.py:125
  83.4 5.8 %copy.116 = f32[624,2,2,512]{3,0,1,2:T(8,128)} copy(f32[624,2,2,512]{0,3,2,1:T(8,128)} %bitcast.107) | data formatting | bytes 10223616 | tf_op jit(solution)/shard_map/convert_element_type | solution.py:125
  89.3 3.0 fusion.2
  92.3 4.1 %copy.117 = bf16[624,2,2,512]{3,2,1,0:T(2,128)(2,1)} copy(bf16[624,2,2,512]{3,0,2,1:T(8,128)(2,1)S(1)} %fusion.2) | data formatting | bytes 5111808 | tf_op jit(solution)/shard_map/convert_element_type | solution.py:129
  96.4 7.1 %reshape.453 = bf16[13,48,2048,1]{2,1,0,3:T(8,128)(2,1)} reshape(bf16[624,2,2,512]{3,2,1,0:T(2,128)(2,1)} %copy.117) | data formatting | bytes 5111808 | tf_op jit(solution)/shard_map/convert_element_type | solution.py:129
  103.4 8.0 %reshape.424 = f32[13,48,2048]{2,1,0:T(8,128)} reshape(f32[624,2,2,512]{3,2,1,0:T(2,128)} %copy.115) | data formatting | bytes 10223616 | tf_op jit(solution)/shard_map/convert_element_type | solution.py:125
  111.4 3.3 fusion.9
  114.8 1.6 fusion.29
  116.4 3.2 fusion.1
  120.3 1.5 fusion.4
  125.7 3.8 %fusion.44 = f32[624,2048]{1,0:T(8,128)} fusion(bf16[624,512]{1,0:T(8,128)(2,1)S(1)} %bitcast.117, bf16[512,2048]{0,1:T(8,128)(2,1)S(1)} %bitcast.112), kind=kOutput, calls=%fused_computation.103 | convolution fusion | flops 1308622848 | bytes 7847936 | tf_op jit(solution)/shard_map/dot_general | solution.py:165
  129.6 13.2 %reduce-scatter.5.cloned.1.call-done = f32[624,1024]{1,0:T(8,128)} async-done(((f32[624,2048]{1,0:T(8,128)}), f32[624,1024]{1,0:T(8,128)}) %reduce-scatter.5.cloned.1.call-update) | async-done | bytes 2555920 | tf_op jit(solution)/shard_map/reduce_scatter | solution.py:54
  143.6 39.5 %reduce-scatter.7.cloned.1.call-done = f32[624,512]{1,0:T(8,128)} async-done(((f32[624,1024]{1,0:T(8,128)}), f32[624,512]{1,0:T(8,128)}) %reduce-scatter.7.cloned.1.call-update) | async-done | bytes 1277968 | tf_op jit(solution)/shard_map/reduce_scatter | solution.py:55
  183.1 1.6 multiply_reduce_fusion.1
  184.7 5.8 %psum.7 = f32[624,1]{0,1:T(1,128)S(1)} all-reduce(f32[624,1]{0,1:T(1,128)S(1)} %broadcast_in_dim.128), channel_id=1, replica_groups=mesh['req'=8,'kvy'=2,'core'=2] {'kvy','core'}, use_global_device_ids=true, to_apply=%region_6.7 | all-reduce | flops 624 | bytes 4992 | tf_op jit(solution)/shard_map/psum | solution.py:59
  191.6 25.1 %all-gather.9.cloned.1.call-done = bf16[624,1024]{1,0:T(8,128)(2,1)} async-done(((bf16[624,512]{1,0:T(8,128)(2,1)}), bf16[624,1024]{1,0:T(8,128)(2,1)}) %all-gather.9.cloned.1.call-update) | async-done | bytes 1277968 | tf_op jit(solution)/shard_map/all_gather | solution.py:40
  216.8 6.6 %copy.123 = bf16[1024,2048]{0,1:T(8,128)(2,1)} copy(bf16[1024,2048]{1,0:T(8,128)(2,1)} %param.27) | data formatting | bytes 8388608 | tf_op args[12]
  223.4 5.1 %copy.124 = bf16[1024,2,2,512]{0,3,2,1:T(8,128)(2,1)} copy(bf16[1024,2,2,512]{0,3,1,2:T(8,128)(2,1)} %bitcast.108) | data formatting | bytes 8388608 | tf_op jit(solution)/shard_map/transpose | solution.py:50
  229.4 7.1 %reshape.417 = bf16[624,2,2,512]{3,2,1,0:T(2,128)(2,1)} reshape(bf16[624,2048]{1,0:T(8,128)(2,1)} %all-gather.11.cloned.1.call-done) | data formatting | bytes 5111808 | tf_op jit(solution)/shard_map/reshape | solution.py:42
  236.5 7.5 %copy.122 = bf16[624,2,2,512]{0,3,1,2:T(8,128)(2,1)} copy(bf16[624,2,2,512]{3,2,1,0:T(2,128)(2,1)} %reshape.417) | data formatting | bytes 5111808 | tf_op jit(solution)/shard_map/reshape | solution.py:42
  244.0 7.3 %fusion.45 = f32[624,1024]{1,0:T(8,128)} fusion(bf16[624,2048]{0,1:T(8,128)(2,1)} %bitcast.118, bf16[2048,1024]{1,0:T(8,128)(2,1)} %param.25), kind=kOutput, calls=%fused_computation.104 | convolution fusion | flops 2617245696 | bytes 9306112 | tf_op jit(solution)/shard_map/dot_general | solution.py:171
  251.4 13.0 %fusion.19 = f32[624,2048]{1,0:T(8,128)} fusion(bf16[1024,2048]{0,1:T(8,128)(2,1)} %bitcast.115, f32[624,1024]{1,0:T(8,128)} %fusion.45, bf16[624,2048]{0,1:T(8,128)(2,1)} %bitcast.119, bf16[2048,1024]{1,0:T(8,128)(2,1)} %param.26), kind=kOutput, calls=%fused_computation.39 | convolution fusion | flops 5238325248 | bytes 18612224 | tf_op jit(solution)/shard_map/dot_general | solution.py:175
  264.5 14.3 %reduce-scatter.9.cloned.1.call-done = f32[624,1024]{1,0:T(8,128)} async-done(((f32[624,2048]{1,0:T(8,128)}), f32[624,1024]{1,0:T(8,128)}) %reduce-scatter.9.cloned.1.call-update) | async-done | bytes 2555920 | tf_op jit(solution)/shard_map/reduce_scatter | solution.py:54
  280.8 5.8 %all-to-all-start.1 = ((s32[8,1,2]{2,1,0:T(1,128)}), s32[8,1,2]{2,1,0:T(1,128)S(1)}, u32[]{:S(2)}, u32[]{:S(2)}) async-start(s32[8,1,2]{2,1,0:T(1,128)} %bitcast.38), calls=%async_computation.5 | async-start | bytes 8192 | tf_op jit(solution)/shard_map/all_to_all | solution.py:117
  286.8 1.6 gather_fusion.1
  288.4 1.5 copy.126
  290.2 1.1 copy.127
  291.3 1.8 all-to-all-done.1
  293.0 4.2 %all-to-all-start.2 = ((bf16[2,8,2,64,256]{4,3,2,0,1:T(8,128)(2,1)}), bf16[2,8,2,64,256]{4,3,2,0,1:T(8,128)(2,1)S(1)}, u32[]{:S(2)}, u32[]{:S(2)}) async-start(bf16[2,8,2,64,256]{4,3,2,0,1:T(8,128)(2,1)} %copy.127), calls=%async_computation.6 | async-start | bytes 2097152 | tf_op jit(solution)/shard_map/all_to_all | solution.py:116
  298.9 24.1 %all-to-all-done.2 = bf16[2,8,2,64,256]{4,3,2,0,1:T(8,128)(2,1)S(1)} async-done(((bf16[2,8,2,64,256]{4,3,2,0,1:T(8,128)(2,1)}), bf16[2,8,2,64,256]{4,3,2,0,1:T(8,128)(2,1)S(1)}, u32[]{:S(2)}, u32[]{:S(2)}) %all-to-all-start.2) | async-done | bytes 1048608 | tf_op jit(solution)/shard_map/all_to_all | solution.py:116
  323.0 1.1 copy.128
  324.1 2.7 gather_fusion.2
  326.8 1.4 select_bitcast_fusion
  329.2 2.3 select_convert_fusion
  (102 shorter events, 15.9 us)
Async XLA Ops:
  7.2 104.3 %copy-start = (bf16[2048,256]{1,0:T(8,128)(2,1)S(1)}, bf16[2048,256]{1,0:T(8,128)(2,1)}, u32[]{:S(2)}) copy-start(bf16[2048,256]{1,0:T(8,128)(2,1)} %param.21) | copy-start | bytes 3145732
  7.2 31.1 %copy-start.11 = (bf16[13,16,1024]{2,1,0:T(8,128)(2,1)S(1)}, bf16[13,16,1024]{2,1,0:T(8,128)(2,1)}, u32[]{:S(2)}) copy-start(bf16[13,16,1024]{2,1,0:T(8,128)(2,1)} %param.28) | copy-start | bytes 1277956
  7.2 29.0 %all-gather.5.cloned.1.call-start = ((), (), s32[]{:S(2)}) async-start(), calls=%async_computation.7 | async-start | bytes 1916928 | tf_op jit(solution)/shard_map/all_gather | solution.py:40
  7.9 53.6 %all-gather.7.cloned.1.call-start = ((), (), s32[]{:S(2)}) async-start(), calls=%async_computation.8 | async-start | bytes 3833856 | tf_op jit(solution)/shard_map/all_gather | solution.py:41
  39.4 7.4 %copy-start.12 = (f32[2048]{0:T(1024)S(1)}, f32[2048]{0:T(1024)}, u32[]{:S(2)}) copy-start(f32[2048]{0:T(1024)} %param.19) | copy-start | bytes 24580
  39.4 7.5 %copy-start.9 = (bf16[2048,512]{1,0:T(8,128)(2,1)S(1)}, bf16[2048,512]{1,0:T(8,128)(2,1)}, u32[]{:S(2)}) copy-start(bf16[2048,512]{1,0:T(8,128)(2,1)} %param.20) | copy-start | bytes 6291460
  42.3 7.0 %copy-start.15 = (s32[13]{0:T(128)S(1)}, s32[13]{0:T(128)}, u32[]{:S(2)}) copy-start(s32[13]{0:T(128)} %param.17) | copy-start | bytes 160
  42.3 16.8 %all-to-all-start = ((bf16[2,4,13,16,256]{4,3,2,0,1:T(8,128)(2,1)}), bf16[2,4,13,16,256]{4,3,2,0,1:T(8,128)(2,1)}, u32[]{:S(2)}, u32[]{:S(2)}) async-start(bf16[2,4,13,16,256]{4,3,2,0,1:T(8,128)(2,1)} %copy.111), calls=%async_computation | async-start | bytes 1703936 | tf_op jit(solution)/shard_map/all_to_all | solution.py:96
  46.7 96.0 %reduce-scatter.5.cloned.1.call-start = ((), (), s32[]{:S(2)}) async-start(), calls=%async_computation.9 | async-start | bytes 7667712 | tf_op jit(solution)/shard_map/reduce_scatter | solution.py:54
  52.2 1.6 copy-start.13
  60.4 1.0 copy-start.5
  116.3 3.3 copy-start.8
  116.4 3.9 %copy-start.10 = (bf16[512,2048]{1,0:T(8,128)(2,1)S(1)}, bf16[512,2048]{1,0:T(8,128)(2,1)}, u32[]{:S(2)}) copy-start(bf16[512,2048]{1,0:T(8,128)(2,1)} %copy.132) | copy-start | bytes 6291460
  122.0 1.2 copy-start.14
  124.1 1.6 copy-start.7
  129.5 53.6 %copy-start.4 = (bf16[624,512]{1,0:T(8,128)(2,1)S(1)}, bf16[624,512]{1,0:T(8,128)(2,1)}, u32[]{:S(2)}) copy-start(bf16[624,512]{1,0:T(8,128)(2,1)} %param.15) | copy-start | bytes 1916932
  129.5 53.5 %reduce-scatter.7.cloned.1.call-start = ((), (), s32[]{:S(2)}) async-start(), calls=%async_computation.10 | async-start | bytes 3833856 | tf_op jit(solution)/shard_map/reduce_scatter | solution.py:55
  142.8 74.0 %all-gather.9.cloned.1.call-start = ((), (), s32[]{:S(2)}) async-start(), calls=%async_computation.11 | async-start | bytes 1916928 | tf_op jit(solution)/shard_map/all_gather | solution.py:40
  183.1 7.5 %copy-start.3 = (f32[624,512]{1,0:T(8,128)S(1)}, f32[624,512]{1,0:T(8,128)}, u32[]{:S(2)}) copy-start(f32[624,512]{1,0:T(8,128)} %reduce-scatter.7.cloned.1.call-done) | copy-start | bytes 3833860
  191.6 37.8 %all-gather.11.cloned.1.call-start = ((), (), s32[]{:S(2)}) async-start(), calls=%async_computation.12 | async-start | bytes 3833856 | tf_op jit(solution)/shard_map/all_gather | solution.py:41
  216.8 62.0 %reduce-scatter.9.cloned.1.call-start = ((), (), s32[]{:S(2)}) async-start(), calls=%async_computation.13 | async-start | bytes 7667712 | tf_op jit(solution)/shard_map/reduce_scatter | solution.py:54
  264.4 14.4 %copy-start.2 = (s32[13]{0:T(128)S(1)}, s32[13]{0:T(128)}, u32[]{:S(2)}) copy-start(s32[13]{0:T(128)} %param.18) | copy-start | bytes 160
  264.4 22.4 %copy-start.6 = (bf16[2,4,13,16,256]{4,3,1,2,0:T(8,128)(2,1)S(1)}, bf16[2,4,13,16,256]{4,3,1,2,0:T(8,128)(2,1)}, u32[]{:S(2)}) copy-start(bf16[2,4,13,16,256]{4,3,1,2,0:T(8,128)(2,1)} %copy-done.5) | copy-start | bytes 2555908
  264.4 64.7 %reduce-scatter.11.cloned.1.call-start = ((), (), s32[]{:S(2)}) async-start(), calls=%async_computation.14 | async-start | bytes 3833856 | tf_op jit(solution)/shard_map/reduce_scatter | solution.py:55
  280.8 12.2 %all-to-all-start.1 = ((s32[8,1,2]{2,1,0:T(1,128)}), s32[8,1,2]{2,1,0:T(1,128)S(1)}, u32[]{:S(2)}, u32[]{:S(2)}) async-start(s32[8,1,2]{2,1,0:T(1,128)} %bitcast.38), calls=%async_computation.5 | async-start | bytes 8192 | tf_op jit(solution)/shard_map/all_to_all | solution.py:117
  293.0 29.9 %all-to-all-start.2 = ((bf16[2,8,2,64,256]{4,3,2,0,1:T(8,128)(2,1)}), bf16[2,8,2,64,256]{4,3,2,0,1:T(8,128)(2,1)S(1)}, u32[]{:S(2)}, u32[]{:S(2)}) async-start(bf16[2,8,2,64,256]{4,3,2,0,1:T(8,128)(2,1)} %copy.127), calls=%async_computation.6 | async-start | bytes 2097152 | tf_op jit(solution)/shard_map/all_to_all | solution.py:116
  326.8 4.7 %copy-start.1 = (bf16[2048,256]{1,0:T(8,128)(2,1)S(1)}, bf16[2048,256]{1,0:T(8,128)(2,1)}, u32[]{:S(2)}) copy-start(bf16[2048,256]{1,0:T(8,128)(2,1)} %param.21) | copy-start | bytes 3145732
Sparse Core Ops, SparseCore 0:
  9.6 26.5 all-gather.4
  37.7 11.5 all-gather.6
  129.6 13.0 reduce-scatter.4
  144.9 38.0 reduce-scatter.6
  191.7 24.9 all-gather.8
  218.1 11.2 all-gather.10
  264.5 14.2 reduce-scatter.8
  281.1 38.1 reduce-scatter.10
where the time goes:
time: 340 us; the launch traced here: 338 us
  waiting for transfers between devices  152 us (45%)
  local copies, waits for them, and re-layouts  97.2 us (29%)
  matrix products  30.8 us (9%)
  other arithmetic  23.4 us (7%)
  starting transfers between devices  14.7 us (4%)
  between operations  14.5 us (4%)
  blocking collectives  5.76 us (2%)
    all_gather x2, waiting for transfers between devices, gather_features(): pair = lax.all_gather(share, 'kvy', axis=1, tiled=True)  53.3 us
    reduce_scatter x2, waiting for transfers between devices, scatter_features(): return lax.psum_scatter(on_chip, 'kvy', scatter_dimension=1, tiled=True)  39.5 us
    convert_element_type x5, local copies, waits for them, and re-layouts, local(): x_float = x_whole.astype(jnp.float32)  32.7 us
    reduce_scatter x2, waiting for transfers between devices, scatter_features(): on_chip = lax.psum_scatter(partial, 'core', scatter_dimension=1, tiled=True)  27.5 us
    all_to_all x1, waiting for transfers between devices, local(): lax.all_to_all(packed, 'req', split_axis=1, concat_axis=1, tiled=True)  24.1 us
    reshape x2, local copies, waits for them, and re-layouts, gather_features(): whole = whole.reshape(rows, CORES, chips, width).transpose(0, 2, 1, 3)  14.6 us
    dot_general x1, matrix products, local(): jnp.dot(hidden, swap_blocks(down_weight), preferred_element_type=jnp.floa...  13 us
    unnamed x35, local copies, waits for them, and re-layouts  12 us
  transfers between devices with their start and end apart: 11, of which 9 were waited for; matrix products, arithmetic and copies ran while one was open for 13% of the time, Pallas kernels for 0%

commit v1 on v0

--- a/solution.py
+++ b/solution.py
@@ -9,6 +9,17 @@
 CORES = 2
 rope_base = 1000042.0
 epsilon = 1e-05
+
+
+def view_fields(panel, axis_k, local_values):
+    local_out, local_part = (panel.shape[:axis_k], panel.shape[axis_k + 1 :])
+    return jnp.moveaxis(panel.reshape(*local_out, local_values, -1, *local_part), axis_k, 0)
+
+
+def read_inputs(arr, d0):
+    arr = jnp.moveaxis(arr, 0, d0)
+    x_new = arr.shape
+    return arr.reshape(*x_new[:d0], x_new[d0] * x_new[d0 + 1], *x_new[d0 + 2 :])
 
 
 def rotate_pairs(tensor, position):
@@ -114,7 +125,17 @@
     packed = packed.reshape((2, req_count, capacity) + packed.shape[2:])
     packed_slots = jnp.where(filled, jnp.take(decode_slot, picked), -1).reshape(req_count, capacity)
     landed = lax.all_to_all(packed, "req", split_axis=1, concat_axis=1, tiled=True)
-    landed_slots = lax.all_to_all(packed_slots, "req", split_axis=0, concat_axis=0, tiled=True)
+    frame_out, current_arr = (jax.lax.axis_size("req"), jax.lax.axis_index("req"))
+    base_arr = view_fields(packed_slots, 0, frame_out)
+    h_now = base_arr
+    for dev in range(1, frame_out):
+        big, r1 = ((current_arr + dev) % frame_out, (current_arr - dev) % frame_out)
+        new = lax.dynamic_index_in_dim(base_arr, big, 0)
+        out_arr = jax.lax.ppermute(
+            new, "req", perm=[(dev_j, (dev_j + dev) % frame_out) for dev_j in range(frame_out)]
+        )
+        h_now = lax.dynamic_update_slice_in_dim(h_now, out_arr, r1, axis=0)
+    landed_slots = read_inputs(h_now, 0)
     wanted = req_index * request_list + order_ids
     slot_hits = landed_slots.reshape(1, -1) == wanted[:, None]
     entry_ids = jnp.arange(req_count * capacity, dtype=jnp.int32)

time: 340 us -> 334 us (0.982)
  waiting for transfers between devices: 152 us -> 142 us
  starting transfers between devices: 14.7 us -> 20.3 us
    all_to_all x1, waiting for transfers between devices: 24.1 us -> 0.01 us  [local(): lax.all_to_all(packed, 'req', split_axis=1, concat_axis=1, tiled=True)]
    ppermute x0 -> x7, waiting for transfers between devices: none -> 16.1 us  [local(): jax.lax.ppermute(new, 'req', perm=[(dev_j, (dev_j + dev) % frame_out) for...]
    ppermute x0 -> x7, starting transfers between devices: none -> 9.79 us  [local(): jax.lax.ppermute(new, 'req', perm=[(dev_j, (dev_j + dev) % frame_out) for...]
    all_to_all x1 -> x0, starting transfers between devices: 5.82 us -> none  [local(): lax.all_to_all(packed_slots, 'req', split_axis=0, concat_axis=0, tiled=True)]
  transfers between devices with their start and end apart: 11 -> 17, of which waited for: 9 -> 9; matrix products, arithmetic and copies ran while one was open for 13% -> 12% of each run, Pallas kernels for 0% -> 0%
where the time goes in v1:
time: 334 us; the launch traced here: 332 us
  waiting for transfers between devices  142 us (43%)
  local copies, waits for them, and re-layouts  95.8 us (29%)
  matrix products  30.8 us (9%)
  other arithmetic  22.2 us (7%)
  starting transfers between devices  20.3 us (6%)
  between operations  14.6 us (4%)
  blocking collectives  5.76 us (2%)
    all_gather x2, waiting for transfers between devices, gather_features(): pair = lax.all_gather(share, 'kvy', axis=1, tiled=True)  53.3 us
    reduce_scatter x2, waiting for transfers between devices, scatter_features(): return lax.psum_scatter(on_chip, 'kvy', scatter_dimension=1, tiled=True)  39.5 us
    convert_element_type x5, local copies, waits for them, and re-layouts, local(): x_float = x_whole.astype(jnp.float32)  32.7 us
    reduce_scatter x2, waiting for transfers between devices, scatter_features(): on_chip = lax.psum_scatter(partial, 'core', scatter_dimension=1, tiled=True)  27.5 us
    ppermute x7, waiting for transfers between devices, local(): jax.lax.ppermute(new, 'req', perm=[(dev_j, (dev_j + dev) % frame_out) for...  16.1 us
    reshape x2, local copies, waits for them, and re-layouts, gather_features(): whole = whole.reshape(rows, CORES, chips, width).transpose(0, 2, 1, 3)  14.6 us
    dot_general x1, matrix products, local(): jnp.dot(hidden, swap_blocks(down_weight), preferred_element_type=jnp.floa...  13 us
    unnamed x35, local copies, waits for them, and re-layouts  12.1 us
  transfers between devices with their start and end apart: 17, of which 9 were waited for; matrix products, arithmetic and copies ran while one was open for 12% of the time, Pallas kernels for 0%

profile of v1, /device:TPU:0, one launch (start us, length us, event | category | flops | bytes accessed | tf_op | source)
XLA Modules:
  0.0 331.5 jit_solution(13441504756632972524)
XLA Ops:
  8.0 28.2 %all-gather.5.cloned.1.call-done = bf16[624,1024]{1,0:T(8,128)(2,1)} async-done(((bf16[624,512]{1,0:T(8,128)(2,1)}), bf16[624,1024]{1,0:T(8,128)(2,1)}) %all-gather.5.cloned.1.call-update) | async-done | bytes 1277968 | tf_op jit(solution)/shard_map/all_gather | solution.py:51
  36.2 2.1 stack.10
  39.4 1.9 maximum_bitcast_fusion
  42.4 4.4 %all-to-all-start = ((bf16[2,4,13,16,256]{4,3,2,0,1:T(8,128)(2,1)}), bf16[2,4,13,16,256]{4,3,2,0,1:T(8,128)(2,1)}, u32[]{:S(2)}, u32[]{:S(2)}) async-start(bf16[2,4,13,16,256]{4,3,2,0,1:T(8,128)(2,1)} %copy.107), calls=%async_computation | async-start | bytes 1703936 | tf_op jit(solution)/shard_map/all_to_all | solution.py:107
  46.8 2.5 copy.127
  49.3 2.9 copy.116
  52.2 1.5 copy.117
  55.1 4.1 %all-to-all-done = bf16[2,4,13,16,256]{4,3,2,0,1:T(8,128)(2,1)} async-done(((bf16[2,4,13,16,256]{4,3,2,0,1:T(8,128)(2,1)}), bf16[2,4,13,16,256]{4,3,2,0,1:T(8,128)(2,1)}, u32[]{:S(2)}, u32[]{:S(2)}) %all-to-all-start) | async-done | bytes 852000 | tf_op jit(solution)/shard_map/all_to_all | solution.py:107
  61.5 4.9 %copy.109 = f32[624,2048]{0,1:T(8,128)} copy(bf16[624,2048]{1,0:T(8,128)(2,1)} %all-gather.7.cloned.1.call-done) | data formatting | bytes 7667712 | tf_op jit(solution)/shard_map/convert_element_type | solution.py:146
  66.4 3.0 multiply_reduce_fusion
  69.3 8.9 %copy.111 = f32[624,2,2,512]{3,2,1,0:T(2,128)} copy(f32[624,2,2,512]{0,3,1,2:T(8,128)} %bitcast.106) | data formatting | bytes 10223616 | tf_op jit(solution)/shard_map/convert_element_type | solution.py:146
  78.2 5.1 %copy.110 = f32[624,2,2,512]{0,3,2,1:T(8,128)} copy(f32[624,2,2,512]{0,3,1,2:T(8,128)} %bitcast.107) | data formatting | bytes 10223616 | tf_op jit(solution)/shard_map/convert_element_type | solution.py:146
  83.4 5.8 %copy.112 = f32[624,2,2,512]{3,0,1,2:T(8,128)} copy(f32[624,2,2,512]{0,3,2,1:T(8,128)} %bitcast.108) | data formatting | bytes 10223616 | tf_op jit(solution)/shard_map/convert_element_type | solution.py:146
  89.3 3.0 fusion.2
  92.3 4.1 %copy.113 = bf16[624,2,2,512]{3,2,1,0:T(2,128)(2,1)} copy(bf16[624,2,2,512]{3,0,2,1:T(8,128)(2,1)S(1)} %fusion.2) | data formatting | bytes 5111808 | tf_op jit(solution)/shard_map/convert_element_type | solution.py:150
  96.4 7.1 %reshape.445 = bf16[13,48,2048,1]{2,1,0,3:T(8,128)(2,1)} reshape(bf16[624,2,2,512]{3,2,1,0:T(2,128)(2,1)} %copy.113) | data formatting | bytes 5111808 | tf_op jit(solution)/shard_map/convert_element_type | solution.py:150
  103.5 8.0 %reshape.416 = f32[13,48,2048]{2,1,0:T(8,128)} reshape(f32[624,2,2,512]{3,2,1,0:T(2,128)} %copy.111) | data formatting | bytes 10223616 | tf_op jit(solution)/shard_map/convert_element_type | solution.py:146
  111.4 3.3 %fusion.9 = f32[13,48,1,256]{3,1,0,2:T(8,128)S(1)} fusion(f32[13,48,2048]{2,1,0:T(8,128)} %reshape.416, f32[2048]{0:T(1024)S(1)} %copy-done.12, f32[13,48]{1,0:T(8,128)S(1)} %rsqrt.17, bf16[2048,256]{1,0:T(8,128)(2,1)S(1)} %copy-done), kind=kOutput, calls=%fused_computation.22 | convolution fusion | flops 658145280 | bytes 6810048 | tf_op jit(solution)/shard_map/dot_general | solution.py:158
  114.8 1.6 fusion.29
  116.4 3.2 fusion.1
  120.3 1.5 fusion.4
  125.7 3.8 %fusion.44 = f32[624,2048]{1,0:T(8,128)} fusion(bf16[624,512]{1,0:T(8,128)(2,1)S(1)} %bitcast.118, bf16[512,2048]{0,1:T(8,128)(2,1)S(1)} %bitcast.113), kind=kOutput, calls=%fused_computation.110 | convolution fusion | flops 1308622848 | bytes 7847936 | tf_op jit(solution)/shard_map/dot_general | solution.py:186
  129.6 13.2 %reduce-scatter.5.cloned.1.call-done = f32[624,1024]{1,0:T(8,128)} async-done(((f32[624,2048]{1,0:T(8,128)}), f32[624,1024]{1,0:T(8,128)}) %reduce-scatter.5.cloned.1.call-update) | async-done | bytes 2555920 | tf_op jit(solution)/shard_map/reduce_scatter | solution.py:65
  143.6 39.5 %reduce-scatter.7.cloned.1.call-done = f32[624,512]{1,0:T(8,128)} async-done(((f32[624,1024]{1,0:T(8,128)}), f32[624,512]{1,0:T(8,128)}) %reduce-scatter.7.cloned.1.call-update) | async-done | bytes 1277968 | tf_op jit(solution)/shard_map/reduce_scatter | solution.py:66
  183.1 1.6 multiply_reduce_fusion.1
  184.7 5.8 %psum.7 = f32[624,1]{0,1:T(1,128)S(1)} all-reduce(f32[624,1]{0,1:T(1,128)S(1)} %broadcast_in_dim.128), channel_id=1, replica_groups=mesh['req'=8,'kvy'=2,'core'=2] {'kvy','core'}, use_global_device_ids=true, to_apply=%region_6.7 | all-reduce | flops 624 | bytes 4992 | tf_op jit(solution)/shard_map/psum | solution.py:70
  191.6 25.1 %all-gather.9.cloned.1.call-done = bf16[624,1024]{1,0:T(8,128)(2,1)} async-done(((bf16[624,512]{1,0:T(8,128)(2,1)}), bf16[624,1024]{1,0:T(8,128)(2,1)}) %all-gather.9.cloned.1.call-update) | async-done | bytes 1277968 | tf_op jit(solution)/shard_map/all_gather | solution.py:51
  216.8 6.6 %copy.119 = bf16[1024,2048]{0,1:T(8,128)(2,1)} copy(bf16[1024,2048]{1,0:T(8,128)(2,1)} %param.27) | data formatting | bytes 8388608 | tf_op args[12]
  223.4 5.1 %copy.120 = bf16[1024,2,2,512]{0,3,2,1:T(8,128)(2,1)} copy(bf16[1024,2,2,512]{0,3,1,2:T(8,128)(2,1)} %bitcast.109) | data formatting | bytes 8388608 | tf_op jit(solution)/shard_map/transpose | solution.py:61
  229.4 7.1 %reshape.409 = bf16[624,2,2,512]{3,2,1,0:T(2,128)(2,1)} reshape(bf16[624,2048]{1,0:T(8,128)(2,1)} %all-gather.11.cloned.1.call-done) | data formatting | bytes 5111808 | tf_op jit(solution)/shard_map/reshape | solution.py:53
  236.5 7.5 %copy.118 = bf16[624,2,2,512]{0,3,1,2:T(8,128)(2,1)} copy(bf16[624,2,2,512]{3,2,1,0:T(2,128)(2,1)} %reshape.409) | data formatting | bytes 5111808 | tf_op jit(solution)/shard_map/reshape | solution.py:53
  244.0 7.3 %fusion.45 = f32[624,1024]{1,0:T(8,128)} fusion(bf16[624,2048]{0,1:T(8,128)(2,1)} %bitcast.119, bf16[2048,1024]{1,0:T(8,128)(2,1)} %param.25), kind=kOutput, calls=%fused_computation.111 | convolution fusion | flops 2617245696 | bytes 9306112 | tf_op jit(solution)/shard_map/dot_general | solution.py:192
  251.3 13.0 %fusion.19 = f32[624,2048]{1,0:T(8,128)} fusion(bf16[1024,2048]{0,1:T(8,128)(2,1)} %bitcast.116, f32[624,1024]{1,0:T(8,128)} %fusion.45, bf16[624,2048]{0,1:T(8,128)(2,1)} %bitcast.120, bf16[2048,1024]{1,0:T(8,128)(2,1)} %param.26), kind=kOutput, calls=%fused_computation.39 | convolution fusion | flops 5238325248 | bytes 18612224 | tf_op jit(solution)/shard_map/dot_general | solution.py:196
  264.4 14.3 %reduce-scatter.9.cloned.1.call-done = f32[624,1024]{1,0:T(8,128)} async-done(((f32[624,2048]{1,0:T(8,128)}), f32[624,1024]{1,0:T(8,128)}) %reduce-scatter.9.cloned.1.call-update) | async-done | bytes 2555920 | tf_op jit(solution)/shard_map/reduce_scatter | solution.py:65
  279.4 1.6 gather_fusion.1
  281.0 1.3 copy.121
  283.7 5.8 %all-to-all-start.1 = ((bf16[2,8,2,64,256]{4,3,2,0,1:T(8,128)(2,1)}), bf16[2,8,2,64,256]{4,3,2,0,1:T(8,128)(2,1)}, u32[]{:S(2)}, u32[]{:S(2)}) async-start(bf16[2,8,2,64,256]{4,3,2,0,1:T(8,128)(2,1)} %copy.122), calls=%async_computation.5 | async-start | bytes 2097152 | tf_op jit(solution)/shard_map/all_to_all | solution.py:127
  290.5 2.1 collective-permute-start
  292.5 1.5 collective-permute-start.1
  294.0 2.4 collective-permute-start.2
  296.4 1.5 collective-permute-start.3
  297.8 2.4 collective-permute-start.4
  300.4 11.6 %collective-permute-done = s32[1,1,2]{2,0,1:T(1,128)S(1)} collective-permute-done((s32[1,1,2]{2,0,1:T(1,128)S(1)}, s32[1,1,2]{2,0,1:T(1,128)S(1)}, u32[]{:S(2)}, u32[]{:S(2)}) %collective-permute-start) | collective-permute-done | bytes 40 | tf_op jit(solution)/shard_map/ppermute | solution.py:134
  312.1 4.5 %collective-permute-done.2 = s32[1,1,2]{2,0,1:T(1,128)S(1)} collective-permute-done((s32[1,1,2]{2,0,1:T(1,128)S(1)}, s32[1,1,2]{2,0,1:T(1,128)S(1)}, u32[]{:S(2)}, u32[]{:S(2)}) %collective-permute-start.2) | collective-permute-done | bytes 40 | tf_op jit(solution)/shard_map/ppermute | solution.py:134
  317.1 1.3 copy.123
  318.4 1.5 gather_fusion.2
  320.0 1.4 select_bitcast_fusion
  322.3 2.3 select_convert_fusion
  (120 shorter events, 19.0 us)
Async XLA Ops:
  7.2 104.3 %copy-start = (bf16[2048,256]{1,0:T(8,128)(2,1)S(1)}, bf16[2048,256]{1,0:T(8,128)(2,1)}, u32[]{:S(2)}) copy-start(bf16[2048,256]{1,0:T(8,128)(2,1)} %param.21) | copy-start | bytes 3145732
  7.2 31.1 %copy-start.11 = (bf16[13,16,1024]{2,1,0:T(8,128)(2,1)S(1)}, bf16[13,16,1024]{2,1,0:T(8,128)(2,1)}, u32[]{:S(2)}) copy-start(bf16[13,16,1024]{2,1,0:T(8,128)(2,1)} %param.28) | copy-start | bytes 1277956
  7.2 29.0 %all-gather.5.cloned.1.call-start = ((), (), s32[]{:S(2)}) async-start(), calls=%async_computation.6 | async-start | bytes 1916928 | tf_op jit(solution)/shard_map/all_gather | solution.py:51
  7.9 53.6 %all-gather.7.cloned.1.call-start = ((), (), s32[]{:S(2)}) async-start(), calls=%async_computation.7 | async-start | bytes 3833856 | tf_op jit(solution)/shard_map/all_gather | solution.py:52
  39.4 7.4 %copy-start.12 = (f32[2048]{0:T(1024)S(1)}, f32[2048]{0:T(1024)}, u32[]{:S(2)}) copy-start(f32[2048]{0:T(1024)} %param.19) | copy-start | bytes 24580
  39.4 7.4 %copy-start.9 = (bf16[2048,512]{1,0:T(8,128)(2,1)S(1)}, bf16[2048,512]{1,0:T(8,128)(2,1)}, u32[]{:S(2)}) copy-start(bf16[2048,512]{1,0:T(8,128)(2,1)} %param.20) | copy-start | bytes 6291460
  42.4 6.9 %copy-start.15 = (s32[13]{0:T(128)S(1)}, s32[13]{0:T(128)}, u32[]{:S(2)}) copy-start(s32[13]{0:T(128)} %param.17) | copy-start | bytes 160
  42.4 16.8 %all-to-all-start = ((bf16[2,4,13,16,256]{4,3,2,0,1:T(8,128)(2,1)}), bf16[2,4,13,16,256]{4,3,2,0,1:T(8,128)(2,1)}, u32[]{:S(2)}, u32[]{:S(2)}) async-start(bf16[2,4,13,16,256]{4,3,2,0,1:T(8,128)(2,1)} %copy.107), calls=%async_computation | async-start | bytes 1703936 | tf_op jit(solution)/shard_map/all_to_all | solution.py:107
  46.7 96.0 %reduce-scatter.5.cloned.1.call-start = ((), (), s32[]{:S(2)}) async-start(), calls=%async_computation.8 | async-start | bytes 7667712 | tf_op jit(solution)/shard_map/reduce_scatter | solution.py:65
  52.2 1.6 copy-start.13
  60.4 1.0 copy-start.5
  116.3 3.3 copy-start.8
  116.4 3.9 %copy-start.10 = (bf16[512,2048]{1,0:T(8,128)(2,1)S(1)}, bf16[512,2048]{1,0:T(8,128)(2,1)}, u32[]{:S(2)}) copy-start(bf16[512,2048]{1,0:T(8,128)(2,1)} %copy.127) | copy-start | bytes 6291460
  122.0 1.2 copy-start.14
  124.1 1.6 copy-start.7
  129.5 53.6 %copy-start.4 = (bf16[624,512]{1,0:T(8,128)(2,1)S(1)}, bf16[624,512]{1,0:T(8,128)(2,1)}, u32[]{:S(2)}) copy-start(bf16[624,512]{1,0:T(8,128)(2,1)} %param.15) | copy-start | bytes 1916932
  129.5 53.5 %reduce-scatter.7.cloned.1.call-start = ((), (), s32[]{:S(2)}) async-start(), calls=%async_computation.9 | async-start | bytes 3833856 | tf_op jit(solution)/shard_map/reduce_scatter | solution.py:66
  142.7 74.0 %all-gather.9.cloned.1.call-start = ((), (), s32[]{:S(2)}) async-start(), calls=%async_computation.10 | async-start | bytes 1916928 | tf_op jit(solution)/shard_map/all_gather | solution.py:51
  183.1 7.5 %copy-start.3 = (f32[624,512]{1,0:T(8,128)S(1)}, f32[624,512]{1,0:T(8,128)}, u32[]{:S(2)}) copy-start(f32[624,512]{1,0:T(8,128)} %reduce-scatter.7.cloned.1.call-done) | copy-start | bytes 3833860
  191.6 37.8 %all-gather.11.cloned.1.call-start = ((), (), s32[]{:S(2)}) async-start(), calls=%async_computation.11 | async-start | bytes 3833856 | tf_op jit(solution)/shard_map/all_gather | solution.py:52
  216.7 62.0 %reduce-scatter.9.cloned.1.call-start = ((), (), s32[]{:S(2)}) async-start(), calls=%async_computation.12 | async-start | bytes 7667712 | tf_op jit(solution)/shard_map/reduce_scatter | solution.py:65
  264.4 14.4 %copy-start.2 = (s32[13]{0:T(128)S(1)}, s32[13]{0:T(128)}, u32[]{:S(2)}) copy-start(s32[13]{0:T(128)} %param.18) | copy-start | bytes 160
  264.4 15.1 %copy-start.6 = (bf16[2,4,13,16,256]{4,3,1,2,0:T(8,128)(2,1)S(1)}, bf16[2,4,13,16,256]{4,3,1,2,0:T(8,128)(2,1)}, u32[]{:S(2)}) copy-start(bf16[2,4,13,16,256]{4,3,1,2,0:T(8,128)(2,1)} %copy-done.5) | copy-start | bytes 2555908
  264.4 57.9 %reduce-scatter.11.cloned.1.call-start = ((), (), s32[]{:S(2)}) async-start(), calls=%async_computation.13 | async-start | bytes 3833856 | tf_op jit(solution)/shard_map/reduce_scatter | solution.py:66
  283.7 33.4 %all-to-all-start.1 = ((bf16[2,8,2,64,256]{4,3,2,0,1:T(8,128)(2,1)}), bf16[2,8,2,64,256]{4,3,2,0,1:T(8,128)(2,1)}, u32[]{:S(2)}, u32[]{:S(2)}) async-start(bf16[2,8,2,64,256]{4,3,2,0,1:T(8,128)(2,1)} %copy.122), calls=%async_computation.5 | async-start | bytes 2097152 | tf_op jit(solution)/shard_map/all_to_all | solution.py:127
  290.5 21.5 %collective-permute-start = (s32[1,1,2]{2,0,1:T(1,128)S(1)}, s32[1,1,2]{2,0,1:T(1,128)S(1)}, u32[]{:S(2)}, u32[]{:S(2)}) collective-permute-start(s32[1,1,2]{2,0,1:T(1,128)S(1)} %get-tuple-element.21), channel_id=1, source_target_pairs={{0,4},{4,8},{8,12},{12,16},{16,20},{20,24},{24,28},{28,0},{1,5},{5... | collective-permute-start | bytes 32 | tf_op jit(solution)/shard_map/ppermute | solution.py:134
  292.5 19.5 %collective-permute-start.1 = (s32[1,1,2]{2,0,1:T(1,128)S(1)}, s32[1,1,2]{2,0,1:T(1,128)S(1)}, u32[]{:S(2)}, u32[]{:S(2)}) collective-permute-start(s32[1,1,2]{2,0,1:T(1,128)S(1)} %get-tuple-element.20), channel_id=1, source_target_pairs={{0,8},{4,12},{8,16},{12,20},{16,24},{20,28},{24,0},{28,4},{1,9},{5... | collective-permute-start | bytes 32 | tf_op jit(solution)/shard_map/ppermute | solution.py:134
  294.0 22.6 %collective-permute-start.2 = (s32[1,1,2]{2,0,1:T(1,128)S(1)}, s32[1,1,2]{2,0,1:T(1,128)S(1)}, u32[]{:S(2)}, u32[]{:S(2)}) collective-permute-start(s32[1,1,2]{2,0,1:T(1,128)S(1)} %get-tuple-element.19), channel_id=1, source_target_pairs={{0,12},{4,16},{8,20},{12,24},{16,28},{20,0},{24,4},{28,8},{1,13},{... | collective-permute-start | bytes 32 | tf_op jit(solution)/shard_map/ppermute | solution.py:134
  296.4 20.2 %collective-permute-start.3 = (s32[1,1,2]{2,0,1:T(1,128)S(1)}, s32[1,1,2]{2,0,1:T(1,128)S(1)}, u32[]{:S(2)}, u32[]{:S(2)}) collective-permute-start(s32[1,1,2]{2,0,1:T(1,128)S(1)} %get-tuple-element.18), channel_id=1, source_target_pairs={{0,16},{4,20},{8,24},{12,28},{16,0},{20,4},{24,8},{28,12},{1,17},{... | collective-permute-start | bytes 32 | tf_op jit(solution)/shard_map/ppermute | solution.py:134
  297.8 18.8 %collective-permute-start.4 = (s32[1,1,2]{2,0,1:T(1,128)S(1)}, s32[1,1,2]{2,0,1:T(1,128)S(1)}, u32[]{:S(2)}, u32[]{:S(2)}) collective-permute-start(s32[1,1,2]{2,0,1:T(1,128)S(1)} %get-tuple-element.17), channel_id=1, source_target_pairs={{0,20},{4,24},{8,28},{12,0},{16,4},{20,8},{24,12},{28,16},{1,21},{... | collective-permute-start | bytes 32 | tf_op jit(solution)/shard_map/ppermute | solution.py:134
  312.0 4.7 %collective-permute-start.5 = (s32[1,1,2]{2,0,1:T(1,128)S(1)}, s32[1,1,2]{2,0,1:T(1,128)S(1)}, u32[]{:S(2)}, u32[]{:S(2)}) collective-permute-start(s32[1,1,2]{2,0,1:T(1,128)S(1)} %get-tuple-element.16), channel_id=1, source_target_pairs={{0,24},{4,28},{8,0},{12,4},{16,8},{20,12},{24,16},{28,20},{1,25},{... | collective-permute-start | bytes 32 | tf_op jit(solution)/shard_map/ppermute | solution.py:134
  312.0 4.7 %collective-permute-start.6 = (s32[1,1,2]{2,0,1:T(1,128)S(1)}, s32[1,1,2]{2,0,1:T(1,128)S(1)}, u32[]{:S(2)}, u32[]{:S(2)}) collective-permute-start(s32[1,1,2]{2,0,1:T(1,128)S(1)} %get-tuple-element.15), channel_id=1, source_target_pairs={{0,28},{4,0},{8,4},{12,8},{16,12},{20,16},{24,20},{28,24},{1,29},{... | collective-permute-start | bytes 32 | tf_op jit(solution)/shard_map/ppermute | solution.py:134
  320.0 4.7 %copy-start.1 = (bf16[2048,256]{1,0:T(8,128)(2,1)S(1)}, bf16[2048,256]{1,0:T(8,128)(2,1)}, u32[]{:S(2)}) copy-start(bf16[2048,256]{1,0:T(8,128)(2,1)} %param.21) | copy-start | bytes 3145732
Sparse Core Ops, SparseCore 0:
  9.6 26.5 all-gather.4
  37.7 11.5 all-gather.6
  129.6 13.0 reduce-scatter.4
  144.9 38.0 reduce-scatter.6
  191.7 24.9 all-gather.8
  218.1 11.2 all-gather.10
  264.5 14.2 reduce-scatter.8
  281.1 38.1 reduce-scatter.10
